TPU v7x, 32 devices: a whole 2x2x4 slice. The times are simulated.
32 devices in a mesh: amp: 8 (over y, x, core), int: 4 (over z).
Axes of the slice: x: 2, y: 2, z: 4, core: 2. Of those that a mesh axis runs over, the one named last changes fastest.
Arguments:
- amplitudes: float32 [768, 512], P('int'), may hold values from -6 to 6
- slab_integrals: float32 [512, 51200], P('int', 'amp'), may hold values from -0.25 to 0.25
- cycle_integrals: float32 [96, 800, 512], P('int', 'amp'), may hold values from -0.03125 to 0.03125
- occ_irrep: int32 [96], replicated, may hold values from 0 to 7
- vir_irrep: int32 [800], replicated, may hold values from 0 to 7
Outputs:
- ladder: float32 [768, 51200], P('int', 'amp')
- cycle: float32 [512, 512], P('int', 'amp')
All inputs are finite; a program needn't handle non-finite values.
Results may differ from a plain program's by a relative error of at most 0.00011.
Values sent between devices are 32-bit elements; how exact they have to be, the bound alone decides.
No kernel may reach another device: no remote copies, remote signals or barrier semaphores. Data moves between devices by JAX's collectives and lax.ppermute only.
A program may use at most 64 MiB of HBM per device.

v0:
```python
import jax
import jax.numpy as jnp
from jax import lax
from jax.sharding import PartitionSpec as P

PRECISION = lax.Precision.HIGH


def per_device(amplitudes, slab_integrals, cycle_integrals, occ_irrep, vir_irrep, n_amp, n_int):
    nocc = occ_irrep.shape[0]
    nvir = vir_irrep.shape[0]
    rows, pw = amplitudes.shape
    pw_local = slab_integrals.shape[0]
    i_local = rows // nocc
    ibat = i_local * n_int
    width = slab_integrals.shape[1]
    a_local = width // nvir
    slab = a_local * n_amp
    k_local, c_local, columns = cycle_integrals.shape
    if a_local >= 4:
        sizes = [(a_local - 1) // 2, a_local - 2 - (a_local - 1) // 2, 1, 1]
    elif a_local >= 2:
        sizes = [a_local - 1, 1]
    else:
        sizes = [a_local]
    chunks = len(sizes)
    starts = [sum(sizes[:t]) for t in range(chunks)]
    t_cyc = lax.all_to_all(
        amplitudes.reshape(i_local, nocc, pw), "int", split_axis=1, concat_axis=0, tiled=True
    ).reshape(ibat * k_local, pw)
    w2 = cycle_integrals.transpose(1, 0, 2).reshape(c_local * k_local, columns)
    ladder_chunks = []
    cycle_chunks = []
    for t in range(chunks):
        a_chunk = sizes[t]
        v = lax.slice_in_dim(slab_integrals, starts[t] * nvir, (starts[t] + a_chunk) * nvir, axis=1)
        v_all = lax.all_gather(v, "int", axis=0, tiled=True)
        if t:
            v_all, ladder_chunks[-1], cycle_chunks[-1] = lax.optimization_barrier(
                (v_all, ladder_chunks[-1], cycle_chunks[-1])
            )
        ladder_chunks.append(
            jnp.dot(amplitudes, v_all, precision=PRECISION, preferred_element_type=jnp.float32)
        )
        l_cyc = jnp.dot(t_cyc, v_all, precision=PRECISION, preferred_element_type=jnp.float32)
        l_cyc = l_cyc.reshape(ibat, k_local, a_chunk, n_amp, c_local).transpose(3, 0, 2, 4, 1)
        l_cyc = l_cyc.reshape(n_amp, ibat * a_chunk, c_local * k_local)
        moved = lax.all_to_all(l_cyc, "amp", split_axis=0, concat_axis=0, tiled=True)
        moved = moved.reshape(n_amp * ibat * a_chunk, c_local * k_local)
        cycle_chunks.append(
            jnp.dot(moved, w2, precision=PRECISION, preferred_element_type=jnp.float32)
        )
    ladder = jnp.concatenate(ladder_chunks, axis=1)
    parts = jnp.concatenate(
        [c.reshape(n_amp, ibat, sizes[t], columns) for t, c in enumerate(cycle_chunks)], axis=2
    )
    col_local = columns // n_amp
    parts = parts.transpose(1, 0, 2, 3).reshape(n_int, i_local * slab, n_amp, col_local)
    parts = parts.transpose(0, 2, 1, 3).reshape(n_int * n_amp, i_local * slab, col_local)
    gathered = lax.all_to_all(parts, ("int", "amp"), split_axis=0, concat_axis=0, tiled=True)
    sums = jnp.sum(gathered, axis=0)
    row_start = lax.axis_index("int") * i_local
    batch_labels = lax.dynamic_slice_in_dim(occ_irrep, row_start, i_local, 0)
    slab_labels = vir_irrep[:slab]
    row_labels = jnp.bitwise_xor(batch_labels[:, None], slab_labels[None, :]).reshape(-1)
    col_ids = lax.axis_index("amp") * col_local + jnp.arange(col_local, dtype=jnp.int32)
    col_occ = col_ids // slab
    col_vir = col_ids % slab
    occ_match = col_occ[:, None] == jnp.arange(nocc, dtype=jnp.int32)[None, :]
    vir_match = col_vir[:, None] == jnp.arange(slab, dtype=jnp.int32)[None, :]
    occ_lookup = jnp.sum(jnp.where(occ_match, occ_irrep[None, :], 0), axis=1)
    vir_lookup = jnp.sum(jnp.where(vir_match, slab_labels[None, :], 0), axis=1)
    col_labels = jnp.bitwise_xor(occ_lookup, vir_lookup)
    keep = row_labels[:, None] == col_labels[None, :]
    cycle = jnp.where(keep, sums, jnp.zeros_like(sums))
    return (ladder, cycle)


def solution(mesh):
    n_amp = mesh.shape["amp"]
    n_int = mesh.shape["int"]
    in_specs = (P("int", None), P("int", "amp"), P("int", "amp", None), P(), P())
    out_specs = (P("int", "amp"), P("int", "amp"))

    def body(*args):
        return per_device(*args, n_amp=n_amp, n_int=n_int)

    return jax.shard_map(body, mesh=mesh, in_specs=in_specs, out_specs=out_specs, check_vma=False)
```

profile of v0, /device:TPU:0, one launch (start us, length us, event | category | flops | bytes accessed | tf_op | source)
XLA Modules:
  0.0 353.6 jit_solution(3028213121475945152)
XLA Ops:
  7.2 3.6 %fusion.3 = (f32[128,2400]{1,0:T(8,128)}, f32[128,2400]{1,0:T(8,128)}) fusion(f32[128,6400]{1,0:T(8,128)} %param.6), kind=kLoop, calls=%fused_computation.24 | loop fusion | bytes 4915200 | tf_op jit(solution)/shard_map/slice | solution.py:36
  10.9 0.7 all-gather.5.cloned.1.call-update
  12.1 27.5 %all_to_all.40 = f32[2,96,512]{2,0,1:T(2,128)S(1)} all-to-all(f32[2,96,512]{2,0,1:T(2,128)S(1)} %copy.57), channel_id=1, replica_groups=mesh['amp'=8,'int'=4] {'int'}, dimensions={1} | all-to-all | bytes 786432 | tf_op jit(solution)/shard_map/all_to_all | solution.py:28
  39.7 71.0 %all-gather.7.cloned.1.call-done = f32[512,2400]{1,0:T(8,128)} async-done(((f32[128,2400]{1,0:T(8,128)}), f32[512,2400]{1,0:T(8,128)}) %all-gather.7.cloned.1.call-update) | async-done | bytes 4915216 | tf_op jit(solution)/shard_map/all_gather | solution.py:37
  110.7 5.7 %copy.60 = f32[2400,512]{1,0:T(8,128)} copy(f32[2400,512]{0,1:T(8,128)} %bitcast.79) | data formatting | bytes 9830400 | tf_op jit(solution)/shard_map/dot_general | solution.py:45
  116.4 5.4 %reshape.144 = f32[3,8,100,512,1]{3,2,1,0,4:T(8,128)} reshape(f32[2400,512]{1,0:T(8,128)} %copy.60) | data formatting | bytes 9830400 | tf_op jit(solution)/shard_map/dot_general | solution.py:45
  121.9 4.9 %convolution_bitcast_fusion.2 = f32[8,8,3,100,24]{3,4,0,2,1:T(8,128)S(1)} fusion(f32[8,24,512,1,1]{2,1,4,3,0:T(8,128)S(1)} %bitcast.82, f32[3,8,100,512,1]{3,2,1,0,4:T(8,128)} %reshape.144), kind=kOutput, calls=%fused_computation.2 | convolution fusion | flops 1415577600 | bytes 7151616 | tf_op jit(solution)/shard_map/dot_general | solution.py:45
  126.8 5.6 %copy.61 = f32[8,8,3,100,24]{4,3,2,1,0:T(8,128)} copy(f32[8,8,3,100,24]{3,4,0,2,1:T(8,128)S(1)} %convolution_bitcast_fusion.2) | data formatting | bytes 3686400 | tf_op jit(solution)/shard_map/transpose | solution.py:46
  132.5 7.6 %reshape.126 = f32[8,24,2400]{2,1,0:T(8,128)} reshape(f32[8,8,3,100,24]{4,3,2,1,0:T(8,128)} %copy.61) | data formatting | bytes 3686400 | tf_op jit(solution)/shard_map/reshape | solution.py:47
  140.1 3.8 %all-to-all-start.1 = ((f32[8,24,2400]{2,1,0:T(8,128)}), f32[8,24,2400]{2,1,0:T(8,128)S(1)}, u32[]{:S(2)}, u32[]{:S(2)}) async-start(f32[8,24,2400]{2,1,0:T(8,128)} %reshape.126), calls=%async_computation.1 | async-start | bytes 3735552 | tf_op jit(solution)/shard_map/all_to_all | solution.py:48
  144.1 2.5 fusion.2
  146.6 5.6 %fusion.4 = f32[192,2400]{1,0:T(8,128)} fusion(f32[192,512]{1,0:T(8,128)S(1)} %copy-done.2, f32[512,2400]{1,0:T(8,128)} %all-gather.7.cloned.1.call-done), kind=kOutput, calls=%fused_computation.25 | convolution fusion | flops 1415577600 | bytes 7151616 | tf_op jit(solution)/shard_map/dot_general | solution.py:43
  152.2 15.8 %all-to-all-done.1 = f32[8,24,2400]{2,1,0:T(8,128)S(1)} async-done(((f32[8,24,2400]{2,1,0:T(8,128)}), f32[8,24,2400]{2,1,0:T(8,128)S(1)}, u32[]{:S(2)}, u32[]{:S(2)}) %all-to-all-start.1) | async-done | bytes 1843232 | tf_op jit(solution)/shard_map/all_to_all | solution.py:48
  168.0 5.1 %fusion.5 = f32[192,512]{1,0:T(8,128)} fusion(f32[192,2400]{1,0:T(8,128)S(1)} %bitcast.88, f32[2400,512]{1,0:T(8,128)} %bitcast.74), kind=kOutput, calls=%fused_computation.26 | convolution fusion | flops 1415577600 | bytes 7151616 | tf_op jit(solution)/shard_map/dot_general | solution.py:51
  173.2 32.0 %all-gather.5.cloned.1.call-done = f32[512,2400]{1,0:T(8,128)} async-done(((f32[128,2400]{1,0:T(8,128)}), f32[512,2400]{1,0:T(8,128)}) %all-gather.5.cloned.1.call-update) | async-done | bytes 4915216 | tf_op jit(solution)/shard_map/all_gather | solution.py:37
  205.2 5.5 %convolution_bitcast_fusion = f32[192,2400]{1,0:T(8,128)} fusion(f32[512,2400]{1,0:T(8,128)} %all-gather.5.cloned.1.call-done, f32[192,512]{1,0:T(8,128)S(1)} %bitcast.83), kind=kOutput, calls=%fused_computation | convolution fusion | flops 1415577600 | bytes 7151616 | tf_op jit(solution)/shard_map/dot_general | solution.py:45
  210.6 2.6 reshape.130
  213.3 5.6 %copy.63 = f32[8,24,3,8,100]{1,4,2,0,3:T(8,128)} copy(f32[8,24,3,8,100]{4,3,2,1,0:T(8,128)S(1)} %reshape.130) | data formatting | bytes 3686400 | tf_op jit(solution)/shard_map/reshape | solution.py:46
  218.9 7.6 %reshape.131 = f32[8,24,2400]{2,1,0:T(8,128)} reshape(f32[8,8,3,100,24]{4,3,2,1,0:T(8,128)} %bitcast.78) | data formatting | bytes 3686400 | tf_op jit(solution)/shard_map/reshape | solution.py:47
  226.5 3.6 %all-to-all-start.2 = ((f32[8,24,2400]{2,1,0:T(8,128)}), f32[8,24,2400]{2,1,0:T(8,128)S(1)}, u32[]{:S(2)}, u32[]{:S(2)}) async-start(f32[8,24,2400]{2,1,0:T(8,128)} %reshape.131), calls=%async_computation.2 | async-start | bytes 3735552 | tf_op jit(solution)/shard_map/all_to_all | solution.py:48
  230.6 5.5 %convolution_bitcast_fusion.1 = f32[192,2400]{1,0:T(8,128)} fusion(f32[512,2400]{1,0:T(8,128)} %all-gather.5.cloned.1.call-done, f32[192,512]{1,0:T(8,128)S(1)} %copy-done.2), kind=kOutput, calls=%fused_computation.1 | convolution fusion | flops 1415577600 | bytes 7151616 | tf_op jit(solution)/shard_map/dot_general | solution.py:43
  236.1 18.1 %all-to-all-done.2 = f32[8,24,2400]{2,1,0:T(8,128)S(1)} async-done(((f32[8,24,2400]{2,1,0:T(8,128)}), f32[8,24,2400]{2,1,0:T(8,128)S(1)}, u32[]{:S(2)}, u32[]{:S(2)}) %all-to-all-start.2) | async-done | bytes 1843232 | tf_op jit(solution)/shard_map/all_to_all | solution.py:48
  254.3 5.2 %fusion.6 = f32[192,512]{1,0:T(8,128)} fusion(f32[192,2400]{1,0:T(8,128)S(1)} %bitcast.89, f32[2400,512]{1,0:T(8,128)} %bitcast.75), kind=kOutput, calls=%fused_computation.27 | convolution fusion | flops 1415577600 | bytes 7151616 | tf_op jit(solution)/shard_map/dot_general | solution.py:51
  259.5 2.3 convolution_bitcast_fusion.5
  261.8 1.3 reshape.133
  263.1 2.2 copy.64
  265.3 1.7 reshape.134
  267.1 3.5 %all-to-all-start.3 = ((f32[8,8,2400]{2,1,0:T(8,128)}), f32[8,8,2400]{2,1,0:T(8,128)S(1)}, u32[]{:S(2)}, u32[]{:S(2)}) async-start(f32[8,8,2400]{2,1,0:T(8,128)} %reshape.134), calls=%async_computation.3 | async-start | bytes 1245184 | tf_op jit(solution)/shard_map/all_to_all | solution.py:48
  270.6 3.2 convolution_bitcast_fusion.6
  273.8 7.5 %all-to-all-done.3 = f32[8,8,2400]{2,1,0:T(8,128)S(1)} async-done(((f32[8,8,2400]{2,1,0:T(8,128)}), f32[8,8,2400]{2,1,0:T(8,128)S(1)}, u32[]{:S(2)}, u32[]{:S(2)}) %all-to-all-start.3) | async-done | bytes 614432 | tf_op jit(solution)/shard_map/all_to_all | solution.py:48
  281.3 4.0 %fusion = f32[64,512]{1,0:T(8,128)S(1)} fusion(f32[2400,512]{1,0:T(8,128)} %bitcast.76, f32[8,8,2400]{2,1,0:T(8,128)S(1)} %all-to-all-done.3), kind=kOutput, calls=%fused_computation.9 | convolution fusion | flops 471859200 | bytes 5660672 | tf_op jit(solution)/shard_map/dot_general | solution.py:51
  285.4 3.0 all-gather.11.cloned.1.call-done
  288.3 2.3 convolution_bitcast_fusion.3
  290.7 1.3 reshape.139
  292.0 2.2 copy.65
  294.2 1.7 reshape.140
  295.9 3.9 %all-to-all-start.4 = ((f32[8,8,2400]{2,1,0:T(8,128)}), f32[8,8,2400]{2,1,0:T(8,128)S(1)}, u32[]{:S(2)}, u32[]{:S(2)}) async-start(f32[8,8,2400]{2,1,0:T(8,128)} %reshape.140), calls=%async_computation.4 | async-start | bytes 1245184 | tf_op jit(solution)/shard_map/all_to_all | solution.py:48
  299.9 1.2 reshape.136
  301.3 9.2 %all-to-all-done.4 = f32[8,8,2400]{2,1,0:T(8,128)S(1)} async-done(((f32[8,8,2400]{2,1,0:T(8,128)}), f32[8,8,2400]{2,1,0:T(8,128)S(1)}, u32[]{:S(2)}, u32[]{:S(2)}) %all-to-all-start.4) | async-done | bytes 614432 | tf_op jit(solution)/shard_map/all_to_all | solution.py:48
  310.5 4.0 %convolution_bitcast_fusion.7 = f32[8,8,1,512]{3,1,0,2:T(8,128)S(1)} fusion(f32[8,8,2400]{2,1,0:T(8,128)S(1)} %all-to-all-done.4, f32[2400,512,1]{1,0,2:T(8,128)} %bitcast.77), kind=kOutput, calls=%fused_computation.7 | convolution fusion | flops 471859200 | bytes 5660672 | tf_op jit(solution)/shard_map/dot_general | solution.py:51
  314.7 0.5 maximum_bitcast_fusion
  315.7 1.6 copy.69
  317.3 2.8 all-to-all-start.5
  320.1 0.7 slice.19
  321.4 3.2 convolution_bitcast_fusion.4
  324.6 6.0 %concatenate.6 = f32[192,6400]{1,0:T(8,128)} concatenate(f32[192,2400]{1,0:T(8,128)S(1)} %copy-done.4, f32[192,2400]{1,0:T(8,128)} %convolution_bitcast_fusion.1, f32[192,800]{1,0:T(8,128)} %convolution_bitcast_fusion.6, f32[192,800]{1,0:T(8,128)} %convolution_bitcast_fusion.4), dimensions={1} | concatenate | bytes 9830400 | tf_op jit(solution)/shard_map/concatenate | solution.py:53
  330.6 15.7 %all-to-all-done.5 = f32[32,128,64]{1,2,0:T(8,128)S(1)} async-done(((f32[32,128,64]{1,2,0:T(8,128)}), f32[32,128,64]{1,2,0:T(8,128)S(1)}, u32[]{:S(2)}, u32[]{:S(2)}) %all-to-all-start.5) | async-done | bytes 1048608 | tf_op jit(solution)/shard_map/all_to_all | solution.py:60
  346.4 0.7 compare_select_fusion
  (38 shorter events, 3.2 us)
Async XLA Ops:
  7.2 103.6 %all-gather.7.cloned.1.call-start = ((), (), s32[]{:S(2)}) async-start(), calls=%async_computation.7 | async-start | bytes 6225920 | tf_op jit(solution)/shard_map/all_gather | solution.py:37
  10.8 1.0 copy-start.2
  10.8 194.3 %all-gather.5.cloned.1.call-start = ((), (), s32[]{:S(2)}) async-start(), calls=%async_computation.6 | async-start | bytes 6225920 | tf_op jit(solution)/shard_map/all_gather | solution.py:37
  39.7 219.8 %copy-start = (f32[4,2,24,512]{3,2,1,0:T(8,128)}, f32[4,2,24,512]{3,2,1,0:T(8,128)S(1)}, u32[]{:S(2)}) copy-start(f32[4,2,24,512]{3,2,1,0:T(8,128)S(1)} %copy.59) | copy-start | bytes 1179652
  140.1 28.0 %all-to-all-start.1 = ((f32[8,24,2400]{2,1,0:T(8,128)}), f32[8,24,2400]{2,1,0:T(8,128)S(1)}, u32[]{:S(2)}, u32[]{:S(2)}) async-start(f32[8,24,2400]{2,1,0:T(8,128)} %reshape.126), calls=%async_computation.1 | async-start | bytes 3735552 | tf_op jit(solution)/shard_map/all_to_all | solution.py:48
  143.9 115.6 %all-gather.9.cloned.1.call-start = ((), (), s32[]{:S(2)}) async-start(), calls=%async_computation.8 | async-start | bytes 2293760 | tf_op jit(solution)/shard_map/all_gather | solution.py:37
  226.5 27.8 %all-to-all-start.2 = ((f32[8,24,2400]{2,1,0:T(8,128)}), f32[8,24,2400]{2,1,0:T(8,128)S(1)}, u32[]{:S(2)}, u32[]{:S(2)}) async-start(f32[8,24,2400]{2,1,0:T(8,128)} %reshape.131), calls=%async_computation.2 | async-start | bytes 3735552 | tf_op jit(solution)/shard_map/all_to_all | solution.py:48
  230.1 58.3 %all-gather.11.cloned.1.call-start = ((), (), s32[]{:S(2)}) async-start(), calls=%async_computation.9 | async-start | bytes 2293760 | tf_op jit(solution)/shard_map/all_gather | solution.py:37
  267.1 14.3 %all-to-all-start.3 = ((f32[8,8,2400]{2,1,0:T(8,128)}), f32[8,8,2400]{2,1,0:T(8,128)S(1)}, u32[]{:S(2)}, u32[]{:S(2)}) async-start(f32[8,8,2400]{2,1,0:T(8,128)} %reshape.134), calls=%async_computation.3 | async-start | bytes 1245184 | tf_op jit(solution)/shard_map/all_to_all | solution.py:48
  273.8 14.5 %copy-start.1 = (f32[4,2,24,512]{3,2,1,0:T(8,128)S(1)}, f32[4,2,24,512]{3,2,1,0:T(8,128)}, u32[]{:S(2)}) copy-start(f32[4,2,24,512]{3,2,1,0:T(8,128)} %copy-done) | copy-start | bytes 1179652
  295.9 5.1 %copy-start.5 = (f32[192,512]{1,0:T(8,128)S(1)}, f32[192,512]{1,0:T(8,128)}, u32[]{:S(2)}) copy-start(f32[192,512]{1,0:T(8,128)} %fusion.6) | copy-start | bytes 1179652
  295.9 14.6 %all-to-all-start.4 = ((f32[8,8,2400]{2,1,0:T(8,128)}), f32[8,8,2400]{2,1,0:T(8,128)S(1)}, u32[]{:S(2)}, u32[]{:S(2)}) async-start(f32[8,8,2400]{2,1,0:T(8,128)} %reshape.140), calls=%async_computation.4 | async-start | bytes 1245184 | tf_op jit(solution)/shard_map/all_to_all | solution.py:48
  315.7 5.1 %copy-start.6 = (s32[96]{0:T(128)S(1)}, s32[96]{0:T(128)}, u32[]{:S(2)}) copy-start(s32[96]{0:T(128)} %param.8) | copy-start | bytes 1156
  315.7 5.7 %copy-start.3 = (f32[192,512]{1,0:T(8,128)S(1)}, f32[192,512]{1,0:T(8,128)}, u32[]{:S(2)}) copy-start(f32[192,512]{1,0:T(8,128)} %param.5) | copy-start | bytes 1179652
  317.3 7.3 %copy-start.4 = (f32[192,2400]{1,0:T(8,128)S(1)}, f32[192,2400]{1,0:T(8,128)}, u32[]{:S(2)}) copy-start(f32[192,2400]{1,0:T(8,128)} %fusion.4) | copy-start | bytes 5529604
  317.3 29.0 %all-to-all-start.5 = ((f32[32,128,64]{1,2,0:T(8,128)}), f32[32,128,64]{1,2,0:T(8,128)S(1)}, u32[]{:S(2)}, u32[]{:S(2)}) async-start(f32[32,128,64]{1,2,0:T(8,128)} %bitcast.30), calls=%async_computation.5 | async-start | bytes 2097152 | tf_op jit(solution)/shard_map/all_to_all | solution.py:60
Sparse Core Ops, SparseCore 0:
  11.0 99.7 all-gather.6
  112.3 92.8 all-gather.4
  206.8 39.7 all-gather.8
  248.0 40.2 all-gather.10
where the time goes:
time: 355 us; the launch traced here: 354 us
  waiting for transfers between devices  173 us (49%)
  local copies, waits for them, and re-layouts  68 us (19%)
  matrix products  50.8 us (14%)
  blocking collectives  27.5 us (8%)
  starting transfers between devices  18.2 us (5%)
  between operations  14 us (4%)
    all_gather x4, waiting for transfers between devices, per_device(): v_all = lax.all_gather(v, 'int', axis=0, tiled=True)  106 us
    all_to_all x4, waiting for transfers between devices, per_device(): lax.all_to_all(l_cyc, 'amp', split_axis=0, concat_axis=0, tiled=True)  50.6 us
    all_to_all x1, blocking collectives, per_device(): lax.all_to_all(amplitudes.reshape(i_local, nocc, pw), 'int', split_axis=1...  27.5 us
    reshape x4, local copies, waits for them, and re-layouts, per_device(): l_cyc = l_cyc.reshape(n_amp, ibat * a_chunk, c_local * k_local)  18.7 us
    dot_general x4, matrix products, per_device(): jnp.dot(moved, w2, precision=PRECISION, preferred_element_type=jnp.float32)  18.4 us
    dot_general x4, matrix products, per_device(): jnp.dot(amplitudes, v_all, precision=PRECISION, preferred_element_type=jn...  17.4 us
    all_to_all x1, waiting for transfers between devices, per_device(): lax.all_to_all(parts, ('int', 'amp'), split_axis=0, concat_axis=0, tiled=...  15.7 us
    reshape x6, local copies, waits for them, and re-layouts, per_device(): l_cyc.reshape(ibat, k_local, a_chunk, n_amp, c_local)  15.3 us
  transfers between devices with their start and end apart: 9, of which 8 were waited for; matrix products, arithmetic and copies ran while one was open for 29% of the time, Pallas kernels for 0%

commit v1 on v0

--- a/solution.py
+++ b/solution.py
@@ -34,7 +34,14 @@
     for t in range(chunks):
         a_chunk = sizes[t]
         v = lax.slice_in_dim(slab_integrals, starts[t] * nvir, (starts[t] + a_chunk) * nvir, axis=1)
-        v_all = lax.all_gather(v, "int", axis=0, tiled=True)
+        ring = [v]
+        for hop in range(3):
+            ring.append(lax.ppermute(ring[-1], "int", [(dev, (dev + 1) % 4) for dev in range(4)]))
+        v_all = jnp.roll(
+            jnp.concatenate(ring[::-1], axis=0),
+            (lax.axis_index("int") + 1) * ring[0].shape[0],
+            axis=0,
+        )
         if t:
             v_all, ladder_chunks[-1], cycle_chunks[-1] = lax.optimization_barrier(
                 (v_all, ladder_chunks[-1], cycle_chunks[-1])

time: 355 us -> 396 us (1.12); the launches traced: 354 us -> 388 us
  waiting for transfers between devices: 173 us -> 213 us
  blocking collectives: 27.5 us -> 0 us
  other arithmetic: 1.68 us -> 19 us
  starting transfers between devices: 18.2 us -> 32.8 us
  between operations: 14 us -> 1.23 us
  local copies, waits for them, and re-layouts: 68 us -> 74.4 us
    ppermute x0 -> x12, waiting for transfers between devices: none -> 122 us  [per_device(): lax.ppermute(ring[-1], 'int', [(dev, (dev + 1) % 4) for dev in range(4)])]
    all_gather x4 -> x0, waiting for transfers between devices: 106 us -> none  [per_device(): v_all = lax.all_gather(v, 'int', axis=0, tiled=True)]
    all_to_all x0 -> x1, waiting for transfers between devices: none -> 54 us  [per_device(): lax.all_to_all(amplitudes.reshape(i_local, nocc, pw), 'int', split_axis=1...]
    all_to_all x4, waiting for transfers between devices: 50.6 us -> 19.9 us  [per_device(): lax.all_to_all(l_cyc, 'amp', split_axis=0, concat_axis=0, tiled=True)]
    all_to_all x1 -> x0, blocking collectives: 27.5 us -> none  [per_device(): lax.all_to_all(amplitudes.reshape(i_local, nocc, pw), 'int', split_axis=1...]
    concatenate x0 -> x4, other arithmetic: none -> 17.3 us  [per_device(): jnp.roll(jnp.concatenate(ring[::-1], axis=0), (lax.axis_index('int') + 1)...]
    reshape x6 -> x8, local copies, waits for them, and re-layouts: 15.3 us -> 29.1 us  [per_device(): l_cyc.reshape(ibat, k_local, a_chunk, n_amp, c_local)]
    dot_general x2 -> x0, local copies, waits for them, and re-layouts: 11.1 us -> none  [per_device(): jnp.dot(t_cyc, v_all, precision=PRECISION, preferred_element_type=jnp.flo...]
  transfers between devices with their start and end apart: 9 -> 18, of which waited for: 8 -> 12; matrix products, arithmetic and copies ran while one was open for 29% -> 29% of each run, Pallas kernels for 0% -> 0%
where the time goes in v1:
time: 396 us; the launch traced here: 388 us
  waiting for transfers between devices  213 us (54%)
  local copies, waits for them, and re-layouts  74.4 us (19%)
  matrix products  47.6 us (12%)
  starting transfers between devices  32.8 us (8%)
  other arithmetic  19 us (5%)
    ppermute x12, waiting for transfers between devices, per_device(): lax.ppermute(ring[-1], 'int', [(dev, (dev + 1) % 4) for dev in range(4)])  122 us
    all_to_all x1, waiting for transfers between devices, per_device(): lax.all_to_all(amplitudes.reshape(i_local, nocc, pw), 'int', split_axis=1...  54 us
    reshape x8, local copies, waits for them, and re-layouts, per_device(): l_cyc.reshape(ibat, k_local, a_chunk, n_amp, c_local)  29.1 us
    reshape x4, local copies, waits for them, and re-layouts, per_device(): l_cyc = l_cyc.reshape(n_amp, ibat * a_chunk, c_local * k_local)  20.1 us
    all_to_all x4, waiting for transfers between devices, per_device(): lax.all_to_all(l_cyc, 'amp', split_axis=0, concat_axis=0, tiled=True)  19.9 us
    dot_general x4, matrix products, per_device(): jnp.dot(moved, w2, precision=PRECISION, preferred_element_type=jnp.float32)  19.6 us
    dot_general x4, matrix products, per_device(): jnp.dot(amplitudes, v_all, precision=PRECISION, preferred_element_type=jn...  17.9 us
    concatenate x4, other arithmetic, per_device(): jnp.roll(jnp.concatenate(ring[::-1], axis=0), (lax.axis_index('int') + 1)...  17.3 us
  transfers between devices with their start and end apart: 18, of which 12 were waited for; matrix products, arithmetic and copies ran while one was open for 29% of the time, Pallas kernels for 0%

profile of v1, /device:TPU:0, one launch (start us, length us, event | category | flops | bytes accessed | tf_op | source)
XLA Modules:
  0.0 388.1 jit_solution(4929753496661729055)
XLA Ops:
  0.6 2.1 fusion.31
  4.2 3.0 collective-permute-start.3
  9.2 28.1 %collective-permute-done.3 = f32[128,2400]{0,1:T(8,128)} collective-permute-done((f32[128,2400]{0,1:T(8,128)}, f32[128,2400]{0,1:T(8,128)}, u32[]{:S(2)}, u32[]{:S(2)}) %collective-permute-start.3) | collective-permute-done | bytes 1228832 | tf_op jit(solution)/shard_map/ppermute | solution.py:39
  37.4 26.3 %collective-permute-done = f32[128,2400]{0,1:T(8,128)} collective-permute-done((f32[128,2400]{0,1:T(8,128)S(1)}, f32[128,2400]{0,1:T(8,128)}, u32[]{:S(2)}, u32[]{:S(2)}) %collective-permute-start) | collective-permute-done | bytes 1228832 | tf_op jit(solution)/shard_map/ppermute | solution.py:39
  63.7 26.3 %collective-permute-done.4 = f32[128,2400]{0,1:T(8,128)} collective-permute-done((f32[128,2400]{0,1:T(8,128)}, f32[128,2400]{0,1:T(8,128)}, u32[]{:S(2)}, u32[]{:S(2)}) %collective-permute-start.4) | collective-permute-done | bytes 1228832 | tf_op jit(solution)/shard_map/ppermute | solution.py:39
  91.1 5.1 %all-to-all-start = ((f32[2,96,512]{2,0,1:T(2,128)}), f32[2,96,512]{2,0,1:T(2,128)S(1)}, u32[]{:S(2)}, u32[]{:S(2)}) async-start(f32[2,96,512]{2,0,1:T(2,128)} %copy.54), calls=%async_computation | async-start | bytes 786432 | tf_op jit(solution)/shard_map/all_to_all | solution.py:28
  96.2 54.0 %all-to-all-done = f32[2,96,512]{2,0,1:T(2,128)S(1)} async-done(((f32[2,96,512]{2,0,1:T(2,128)}), f32[2,96,512]{2,0,1:T(2,128)S(1)}, u32[]{:S(2)}, u32[]{:S(2)}) %all-to-all-start) | async-done | bytes 393248 | tf_op jit(solution)/shard_map/all_to_all | solution.py:28
  150.4 4.8 %fusion.3 = f32[512,2400]{0,1:T(8,128)S(1)} fusion(s32[]{:T(128)S(6)} %select_n.62, f32[128,2400]{0,1:T(8,128)} %collective-permute-done.5, f32[128,2400]{0,1:T(8,128)} %collective-permute-done.4, f32[128,2400]{0,1:T(8,128)} %collective-permute-done.3, f32[128,2400]{0,1:T(8,128)S(1)} %copy-done.9), kind=kLoop, calls=%fused_computation.19 | loop fusion | flops 8601600 | bytes 9830404 | tf_op jit(solution)/shard_map/jit(_roll_dynamic)/concatenate | solution.py:40
  155.2 2.2 copy-done.1
  157.5 3.8 convolution_bitcast_fusion.2
  161.3 3.6 reshape.126
  164.9 7.2 %copy.57 = f32[8,24,3,8,100]{1,4,2,0,3:T(8,128)} copy(f32[8,24,3,8,100]{4,3,2,1,0:T(8,128)} %reshape.126) | data formatting | bytes 3686400 | tf_op jit(solution)/shard_map/reshape | solution.py:53
  172.1 7.5 %reshape.127 = f32[8,24,2400]{2,1,0:T(8,128)} reshape(f32[8,8,3,100,24]{4,3,2,1,0:T(8,128)} %bitcast.75) | data formatting | bytes 3686400 | tf_op jit(solution)/shard_map/reshape | solution.py:54
  179.7 4.3 %all-to-all-start.1 = ((f32[8,24,2400]{2,1,0:T(8,128)}), f32[8,24,2400]{2,1,0:T(8,128)}, u32[]{:S(2)}, u32[]{:S(2)}) async-start(f32[8,24,2400]{2,1,0:T(8,128)} %reshape.127), calls=%async_computation.1 | async-start | bytes 3735552 | tf_op jit(solution)/shard_map/all_to_all | solution.py:55
  186.2 6.2 %convolution_bitcast_fusion.3 = f32[192,2400]{1,0:T(8,128)} fusion(f32[512,2400]{0,1:T(8,128)} %copy-done.1, f32[192,512]{1,0:T(8,128)S(1)} %copy-done.3), kind=kOutput, calls=%fused_computation.33 | convolution fusion | flops 1415577600 | bytes 7151616 | tf_op jit(solution)/shard_map/dot_general | solution.py:50
  192.4 7.1 %fusion.10 = f32[512,2400]{0,1:T(8,128)} fusion(s32[]{:T(128)S(6)} %select_n.62, f32[128,2400]{0,1:T(8,128)} %collective-permute-done.2, f32[128,2400]{0,1:T(8,128)} %collective-permute-done.1, f32[128,2400]{0,1:T(8,128)} %collective-permute-done, f32[128,2400]{0,1:T(8,128)S(1)} %copy-done.8), kind=kLoop, calls=%fused_computation.26 | loop fusion | flops 8601600 | bytes 9830404 | tf_op jit(solution)/shard_map/jit(_roll_dynamic)/concatenate | solution.py:40
  199.5 8.7 %all-to-all-done.1 = f32[8,24,2400]{2,1,0:T(8,128)} async-done(((f32[8,24,2400]{2,1,0:T(8,128)}), f32[8,24,2400]{2,1,0:T(8,128)}, u32[]{:S(2)}, u32[]{:S(2)}) %all-to-all-start.1) | async-done | bytes 1843232 | tf_op jit(solution)/shard_map/all_to_all | solution.py:55
  208.2 5.8 %fusion.32 = f32[192,512]{1,0:T(8,128)} fusion(f32[192,2400]{1,0:T(8,128)} %bitcast.7, f32[2400,512]{1,0:T(8,128)} %bitcast.71), kind=kOutput, calls=%fused_computation.86 | convolution fusion | flops 1415577600 | bytes 7151616 | tf_op jit(solution)/shard_map/dot_general | solution.py:58
  214.0 3.8 convolution_bitcast_fusion
  217.8 3.6 reshape.130
  221.4 7.2 %copy.58 = f32[8,24,3,8,100]{1,4,2,0,3:T(8,128)} copy(f32[8,24,3,8,100]{4,3,2,1,0:T(8,128)} %reshape.130) | data formatting | bytes 3686400 | tf_op jit(solution)/shard_map/reshape | solution.py:53
  228.6 7.5 %reshape.131 = f32[8,24,2400]{2,1,0:T(8,128)} reshape(f32[8,8,3,100,24]{4,3,2,1,0:T(8,128)} %bitcast.76) | data formatting | bytes 3686400 | tf_op jit(solution)/shard_map/reshape | solution.py:54
  236.2 4.3 %all-to-all-start.2 = ((f32[8,24,2400]{2,1,0:T(8,128)}), f32[8,24,2400]{2,1,0:T(8,128)}, u32[]{:S(2)}, u32[]{:S(2)}) async-start(f32[8,24,2400]{2,1,0:T(8,128)} %reshape.131), calls=%async_computation.2 | async-start | bytes 3735552 | tf_op jit(solution)/shard_map/all_to_all | solution.py:55
  240.8 2.5 collective-permute-start.7
  243.3 12.4 %collective-permute-done.9 = f32[128,800]{1,0:T(8,128)S(1)} collective-permute-done((f32[128,800]{1,0:T(8,128)S(1)}, f32[128,800]{1,0:T(8,128)S(1)}, u32[]{:S(2)}, u32[]{:S(2)}) %collective-permute-start.9) | collective-permute-done | bytes 409632 | tf_op jit(solution)/shard_map/ppermute | solution.py:39
  255.7 9.8 %collective-permute-done.7 = f32[128,800]{1,0:T(8,128)S(1)} collective-permute-done((f32[128,800]{1,0:T(8,128)S(1)}, f32[128,800]{1,0:T(8,128)S(1)}, u32[]{:S(2)}, u32[]{:S(2)}) %collective-permute-start.7) | collective-permute-done | bytes 409632 | tf_op jit(solution)/shard_map/ppermute | solution.py:39
  265.5 9.9 %collective-permute-done.10 = f32[128,800]{1,0:T(8,128)} collective-permute-done((f32[128,800]{1,0:T(8,128)S(1)}, f32[128,800]{1,0:T(8,128)}, u32[]{:S(2)}, u32[]{:S(2)}) %collective-permute-start.10) | collective-permute-done | bytes 409632 | tf_op jit(solution)/shard_map/ppermute | solution.py:39
  275.7 9.6 %collective-permute-done.8 = f32[128,800]{1,0:T(8,128)S(1)} collective-permute-done((f32[128,800]{1,0:T(8,128)S(1)}, f32[128,800]{1,0:T(8,128)S(1)}, u32[]{:S(2)}, u32[]{:S(2)}) %collective-permute-start.8) | collective-permute-done | bytes 409632 | tf_op jit(solution)/shard_map/ppermute | solution.py:39
  285.2 2.3 fusion.24
  287.6 6.9 %convolution_bitcast_fusion.1 = f32[192,2400]{1,0:T(8,128)} fusion(f32[512,2400]{0,1:T(8,128)} %fusion.10, f32[192,512]{1,0:T(8,128)S(1)} %copy-done.3), kind=kOutput, calls=%fused_computation.31 | convolution fusion | flops 1415577600 | bytes 7151616 | tf_op jit(solution)/shard_map/dot_general | solution.py:50
  294.4 5.7 %fusion.33 = f32[192,512]{1,0:T(8,128)} fusion(f32[192,2400]{1,0:T(8,128)} %bitcast.13, f32[2400,512]{1,0:T(8,128)} %bitcast.72), kind=kOutput, calls=%fused_computation.87 | convolution fusion | flops 1415577600 | bytes 7151616 | tf_op jit(solution)/shard_map/dot_general | solution.py:58
  302.2 2.2 copy.59
  306.2 4.4 %all-to-all-start.3 = ((f32[8,8,2400]{2,1,0:T(8,128)}), f32[8,8,2400]{2,1,0:T(8,128)S(1)}, u32[]{:S(2)}, u32[]{:S(2)}) async-start(f32[8,8,2400]{2,1,0:T(8,128)} %reshape.134), calls=%async_computation.3 | async-start | bytes 1245184 | tf_op jit(solution)/shard_map/all_to_all | solution.py:55
  310.6 3.1 fusion.17
  313.7 3.2 convolution_bitcast_fusion.7
  316.9 4.4 %all-to-all-done.3 = f32[8,8,2400]{2,1,0:T(8,128)S(1)} async-done(((f32[8,8,2400]{2,1,0:T(8,128)}), f32[8,8,2400]{2,1,0:T(8,128)S(1)}, u32[]{:S(2)}, u32[]{:S(2)}) %all-to-all-start.3) | async-done | bytes 614432 | tf_op jit(solution)/shard_map/all_to_all | solution.py:55
  321.3 4.0 %fusion.28 = f32[64,512]{1,0:T(8,128)S(1)} fusion(f32[2400,512]{1,0:T(8,128)} %bitcast.73, f32[8,8,2400]{2,1,0:T(8,128)S(1)} %all-to-all-done.3), kind=kOutput, calls=%fused_computation.70 | convolution fusion | flops 471859200 | bytes 5660672 | tf_op jit(solution)/shard_map/dot_general | solution.py:58
  328.6 2.4 copy.60
  331.0 3.3 reshape.140
  334.2 3.5 all-to-all-start.4
  339.0 2.0 reshape.137
  341.7 6.8 %all-to-all-done.4 = f32[8,8,2400]{2,1,0:T(8,128)S(1)} async-done(((f32[8,8,2400]{2,1,0:T(8,128)}), f32[8,8,2400]{2,1,0:T(8,128)S(1)}, u32[]{:S(2)}, u32[]{:S(2)}) %all-to-all-start.4) | async-done | bytes 614432 | tf_op jit(solution)/shard_map/all_to_all | solution.py:55
  348.5 4.1 %convolution_bitcast_fusion.8 = f32[8,8,1,512]{3,1,0,2:T(8,128)S(1)} fusion(f32[8,8,2400]{2,1,0:T(8,128)S(1)} %all-to-all-done.4, f32[2400,512,1]{1,0,2:T(8,128)} %bitcast.74), kind=kOutput, calls=%fused_computation.68 | convolution fusion | flops 471859200 | bytes 5660672 | tf_op jit(solution)/shard_map/dot_general | solution.py:58
  353.4 1.7 reshape.141
  355.1 3.1 copy.64
  358.3 2.6 all-to-all-start.5
  363.9 6.6 %concatenate.28 = f32[192,6400]{1,0:T(8,128)} concatenate(f32[192,2400]{1,0:T(8,128)} %convolution_bitcast_fusion.3, f32[192,2400]{1,0:T(8,128)} %convolution_bitcast_fusion.1, f32[192,800]{1,0:T(8,128)} %convolution_bitcast_fusion.7, f32[192,800]{1,0:T(8,128)} %convolution_bitcast_fusion.5), dimensions={1} | concatenate | bytes 9830400 | tf_op jit(solution)/shard_map/concatenate | solution.py:60
  370.5 16.7 %all-to-all-done.5 = f32[32,128,64]{1,2,0:T(8,128)S(1)} async-done(((f32[32,128,64]{1,2,0:T(8,128)}), f32[32,128,64]{1,2,0:T(8,128)S(1)}, u32[]{:S(2)}, u32[]{:S(2)}) %all-to-all-start.5) | async-done | bytes 1048608 | tf_op jit(solution)/shard_map/all_to_all | solution.py:67
  (72 shorter events, 20.8 us)
Async XLA Ops:
  2.7 87.4 %copy-start.3 = (f32[192,512]{1,0:T(8,128)S(1)}, f32[192,512]{1,0:T(8,128)}, u32[]{:S(2)}) copy-start(f32[192,512]{1,0:T(8,128)} %param.9) | copy-start | bytes 1179652
  4.2 33.2 %collective-permute-start.3 = (f32[128,2400]{0,1:T(8,128)}, f32[128,2400]{0,1:T(8,128)}, u32[]{:S(2)}, u32[]{:S(2)}) collective-permute-start(f32[128,2400]{0,1:T(8,128)} %copy.66), channel_id=1, source_target_pairs={{0,1},{1,2},{2,3},{3,0},{4,5},{5,6},{6,7},{7,4},{8,9},{9,10},{10,1... | collective-permute-start | bytes 3686408 | tf_op jit(solution)/shard_map/ppermute | solution.py:39
  7.6 142.7 %copy-start.7 = (f32[128,2400]{0,1:T(8,128)}, f32[128,2400]{0,1:T(8,128)S(1)}, u32[]{:S(2)}) copy-start(f32[128,2400]{0,1:T(8,128)S(1)} %copy.65) | copy-start | bytes 3686404
  7.6 142.8 %copy-start.9 = (f32[128,2400]{0,1:T(8,128)S(1)}, f32[128,2400]{0,1:T(8,128)}, u32[]{:S(2)}) copy-start(f32[128,2400]{0,1:T(8,128)} %copy.66) | copy-start | bytes 3686404
  7.6 56.1 %collective-permute-start = (f32[128,2400]{0,1:T(8,128)S(1)}, f32[128,2400]{0,1:T(8,128)}, u32[]{:S(2)}, u32[]{:S(2)}) collective-permute-start(f32[128,2400]{0,1:T(8,128)S(1)} %copy.65), channel_id=1, source_target_pairs={{0,1},{1,2},{2,3},{3,0},{4,5},{5,6},{6,7},{7,4},{8,9},{9,10},{10,1... | collective-permute-start | bytes 3686408 | tf_op jit(solution)/shard_map/ppermute | solution.py:39
  37.4 52.7 %collective-permute-start.4 = (f32[128,2400]{0,1:T(8,128)}, f32[128,2400]{0,1:T(8,128)}, u32[]{:S(2)}, u32[]{:S(2)}) collective-permute-start(f32[128,2400]{0,1:T(8,128)} %collective-permute-done.3), channel_id=1, source_target_pairs={{0,1},{1,2},{2,3},{3,0},{4,5},{5,6},{6,7},{7,4},{8,9},{9,10},{10,1... | collective-permute-start | bytes 3686408 | tf_op jit(solution)/shard_map/ppermute | solution.py:39
  63.7 86.6 %collective-permute-start.1 = (f32[128,2400]{0,1:T(8,128)}, f32[128,2400]{0,1:T(8,128)}, u32[]{:S(2)}, u32[]{:S(2)}) collective-permute-start(f32[128,2400]{0,1:T(8,128)} %collective-permute-done), channel_id=1, source_target_pairs={{0,1},{1,2},{2,3},{3,0},{4,5},{5,6},{6,7},{7,4},{8,9},{9,10},{10,1... | collective-permute-start | bytes 3686408 | tf_op jit(solution)/shard_map/ppermute | solution.py:39
  90.0 60.4 %collective-permute-start.5 = (f32[128,2400]{0,1:T(8,128)}, f32[128,2400]{0,1:T(8,128)}, u32[]{:S(2)}, u32[]{:S(2)}) collective-permute-start(f32[128,2400]{0,1:T(8,128)} %collective-permute-done.4), channel_id=1, source_target_pairs={{0,1},{1,2},{2,3},{3,0},{4,5},{5,6},{6,7},{7,4},{8,9},{9,10},{10,1... | collective-permute-start | bytes 3686408 | tf_op jit(solution)/shard_map/ppermute | solution.py:39
  91.1 59.1 %all-to-all-start = ((f32[2,96,512]{2,0,1:T(2,128)}), f32[2,96,512]{2,0,1:T(2,128)S(1)}, u32[]{:S(2)}, u32[]{:S(2)}) async-start(f32[2,96,512]{2,0,1:T(2,128)} %copy.54), calls=%async_computation | async-start | bytes 786432 | tf_op jit(solution)/shard_map/all_to_all | solution.py:28
  150.3 149.8 %copy-start.5 = (f32[4,2,24,512]{3,2,1,0:T(8,128)}, f32[4,2,24,512]{3,2,1,0:T(8,128)S(1)}, u32[]{:S(2)}) copy-start(f32[4,2,24,512]{3,2,1,0:T(8,128)S(1)} %copy.56) | copy-start | bytes 1179652
  150.3 42.1 %collective-permute-start.2 = (f32[128,2400]{0,1:T(8,128)}, f32[128,2400]{0,1:T(8,128)}, u32[]{:S(2)}, u32[]{:S(2)}) collective-permute-start(f32[128,2400]{0,1:T(8,128)} %collective-permute-done.1), channel_id=1, source_target_pairs={{0,1},{1,2},{2,3},{3,0},{4,5},{5,6},{6,7},{7,4},{8,9},{9,10},{10,1... | collective-permute-start | bytes 3686408 | tf_op jit(solution)/shard_map/ppermute | solution.py:39
  155.2 2.3 copy-start.1
  179.7 28.5 %all-to-all-start.1 = ((f32[8,24,2400]{2,1,0:T(8,128)}), f32[8,24,2400]{2,1,0:T(8,128)}, u32[]{:S(2)}, u32[]{:S(2)}) async-start(f32[8,24,2400]{2,1,0:T(8,128)} %reshape.127), calls=%async_computation.1 | async-start | bytes 3735552 | tf_op jit(solution)/shard_map/all_to_all | solution.py:55
  185.5 55.0 %copy-start.11 = (f32[128,800]{1,0:T(8,128)}, f32[128,800]{1,0:T(8,128)S(1)}, u32[]{:S(2)}) copy-start(f32[128,800]{1,0:T(8,128)S(1)} %get-tuple-element.22) | copy-start | bytes 1228804
  185.5 6.9 %copy-start.8 = (f32[128,2400]{0,1:T(8,128)S(1)}, f32[128,2400]{0,1:T(8,128)}, u32[]{:S(2)}) copy-start(f32[128,2400]{0,1:T(8,128)} %copy-done.7) | copy-start | bytes 3686404
  185.5 55.3 %collective-permute-start.6 = (f32[128,800]{1,0:T(8,128)S(1)}, f32[128,800]{1,0:T(8,128)S(1)}, u32[]{:S(2)}, u32[]{:S(2)}) collective-permute-start(f32[128,800]{1,0:T(8,128)S(1)} %get-tuple-element.23), channel_id=1, source_target_pairs={{0,1},{1,2},{2,3},{3,0},{4,5},{5,6},{6,7},{7,4},{8,9},{9,10},{10,1... | collective-permute-start | bytes 1228808 | tf_op jit(solution)/shard_map/ppermute | solution.py:39
  208.2 5.8 %copy-start = (f32[512,2400]{0,1:T(8,128)S(1)}, f32[512,2400]{0,1:T(8,128)}, u32[]{:S(2)}) copy-start(f32[512,2400]{0,1:T(8,128)} %fusion.10) | copy-start | bytes 14745604
  236.2 58.2 %all-to-all-start.2 = ((f32[8,24,2400]{2,1,0:T(8,128)}), f32[8,24,2400]{2,1,0:T(8,128)}, u32[]{:S(2)}, u32[]{:S(2)}) async-start(f32[8,24,2400]{2,1,0:T(8,128)} %reshape.131), calls=%async_computation.2 | async-start | bytes 3735552 | tf_op jit(solution)/shard_map/all_to_all | solution.py:55
  240.5 15.2 %collective-permute-start.9 = (f32[128,800]{1,0:T(8,128)S(1)}, f32[128,800]{1,0:T(8,128)S(1)}, u32[]{:S(2)}, u32[]{:S(2)}) collective-permute-start(f32[128,800]{1,0:T(8,128)S(1)} %get-tuple-element.22), channel_id=1, source_target_pairs={{0,1},{1,2},{2,3},{3,0},{4,5},{5,6},{6,7},{7,4},{8,9},{9,10},{10,1... | collective-permute-start | bytes 1228808 | tf_op jit(solution)/shard_map/ppermute | solution.py:39
  240.8 24.8 %collective-permute-start.7 = (f32[128,800]{1,0:T(8,128)S(1)}, f32[128,800]{1,0:T(8,128)S(1)}, u32[]{:S(2)}, u32[]{:S(2)}) collective-permute-start(f32[128,800]{1,0:T(8,128)S(1)} %collective-permute-done.6), channel_id=1, source_target_pairs={{0,1},{1,2},{2,3},{3,0},{4,5},{5,6},{6,7},{7,4},{8,9},{9,10},{10,1... | collective-permute-start | bytes 1228808 | tf_op jit(solution)/shard_map/ppermute | solution.py:39
  255.7 19.9 %copy-start.13 = (f32[128,800]{1,0:T(8,128)}, f32[128,800]{1,0:T(8,128)S(1)}, u32[]{:S(2)}) copy-start(f32[128,800]{1,0:T(8,128)S(1)} %collective-permute-done.9) | copy-start | bytes 1228804
  255.7 19.8 %collective-permute-start.10 = (f32[128,800]{1,0:T(8,128)S(1)}, f32[128,800]{1,0:T(8,128)}, u32[]{:S(2)}, u32[]{:S(2)}) collective-permute-start(f32[128,800]{1,0:T(8,128)S(1)} %collective-permute-done.9), channel_id=1, source_target_pairs={{0,1},{1,2},{2,3},{3,0},{4,5},{5,6},{6,7},{7,4},{8,9},{9,10},{10,1... | collective-permute-start | bytes 1228808 | tf_op jit(solution)/shard_map/ppermute | solution.py:39
  265.5 19.7 %collective-permute-start.8 = (f32[128,800]{1,0:T(8,128)S(1)}, f32[128,800]{1,0:T(8,128)S(1)}, u32[]{:S(2)}, u32[]{:S(2)}) collective-permute-start(f32[128,800]{1,0:T(8,128)S(1)} %collective-permute-done.7), channel_id=1, source_target_pairs={{0,1},{1,2},{2,3},{3,0},{4,5},{5,6},{6,7},{7,4},{8,9},{9,10},{10,1... | collective-permute-start | bytes 1228808 | tf_op jit(solution)/shard_map/ppermute | solution.py:39
  275.5 35.1 %collective-permute-start.11 = (f32[128,800]{1,0:T(8,128)}, f32[128,800]{1,0:T(8,128)}, u32[]{:S(2)}, u32[]{:S(2)}) collective-permute-start(f32[128,800]{1,0:T(8,128)} %collective-permute-done.10), channel_id=1, source_target_pairs={{0,1},{1,2},{2,3},{3,0},{4,5},{5,6},{6,7},{7,4},{8,9},{9,10},{10,1... | collective-permute-start | bytes 1228808 | tf_op jit(solution)/shard_map/ppermute | solution.py:39
  287.5 12.5 %copy-start.2 = (f32[512,800]{1,0:T(8,128)}, f32[512,800]{1,0:T(8,128)S(1)}, u32[]{:S(2)}) copy-start(f32[512,800]{1,0:T(8,128)S(1)} %fusion.24) | copy-start | bytes 4915204
  306.1 7.5 %copy-start.4 = (f32[192,512]{1,0:T(8,128)S(1)}, f32[192,512]{1,0:T(8,128)}, u32[]{:S(2)}) copy-start(f32[192,512]{1,0:T(8,128)} %param.9) | copy-start | bytes 1179652
  306.2 15.2 %all-to-all-start.3 = ((f32[8,8,2400]{2,1,0:T(8,128)}), f32[8,8,2400]{2,1,0:T(8,128)S(1)}, u32[]{:S(2)}, u32[]{:S(2)}) async-start(f32[8,8,2400]{2,1,0:T(8,128)} %reshape.134), calls=%async_computation.3 | async-start | bytes 1245184 | tf_op jit(solution)/shard_map/all_to_all | solution.py:55
  313.7 11.7 %copy-start.6 = (f32[4,2,24,512]{3,2,1,0:T(8,128)S(1)}, f32[4,2,24,512]{3,2,1,0:T(8,128)}, u32[]{:S(2)}) copy-start(f32[4,2,24,512]{3,2,1,0:T(8,128)} %copy-done.5) | copy-start | bytes 1179652
  334.2 14.3 %all-to-all-start.4 = ((f32[8,8,2400]{2,1,0:T(8,128)}), f32[8,8,2400]{2,1,0:T(8,128)S(1)}, u32[]{:S(2)}, u32[]{:S(2)}) async-start(f32[8,8,2400]{2,1,0:T(8,128)} %reshape.140), calls=%async_computation.4 | async-start | bytes 1245184 | tf_op jit(solution)/shard_map/all_to_all | solution.py:55
  341.7 11.1 %copy-start.12 = (f32[8,8,1,512]{3,2,1,0:T(1,128)S(1)}, f32[8,8,1,512]{3,2,1,0:T(1,128)}, u32[]{:S(2)}) copy-start(f32[8,8,1,512]{3,2,1,0:T(1,128)} %copy.61) | copy-start | bytes 393220
  348.5 4.2 %copy-start.10 = (f32[8,8,3,512]{3,2,1,0:T(4,128)S(1)}, f32[8,8,3,512]{3,2,1,0:T(4,128)}, u32[]{:S(2)}) copy-start(f32[8,8,3,512]{3,2,1,0:T(4,128)} %reshape.137) | copy-start | bytes 1179652
  353.4 8.2 %copy-start.14 = (s32[96]{0:T(128)S(1)}, s32[96]{0:T(128)}, u32[]{:S(2)}) copy-start(s32[96]{0:T(128)} %param.12) | copy-start | bytes 1156
  358.3 28.9 %all-to-all-start.5 = ((f32[32,128,64]{1,2,0:T(8,128)}), f32[32,128,64]{1,2,0:T(8,128)S(1)}, u32[]{:S(2)}, u32[]{:S(2)}) async-start(f32[32,128,64]{1,2,0:T(8,128)} %bitcast.27), calls=%async_computation.5 | async-start | bytes 2097152 | tf_op jit(solution)/shard_map/all_to_all | solution.py:67
